TPU v7x, 32 devices: a whole 2x2x4 slice. The times are simulated.
32 devices in a mesh: dp: 8 (over z, y), feat: 4 (over x, core).
Axes of the slice: x: 2, y: 2, z: 4, core: 2. Of those that a mesh axis runs over, the one named last changes fastest.
Arguments:
- activations: bfloat16 [16384, 2048], P('feat', 'dp'), may hold values from -6 to 6
- cotangent: bfloat16 [16384, 2048], P('feat', 'dp'), may hold values from -6 to 6
- r_mix: bfloat16 [64, 256, 256], P('feat', 'dp'), may hold values from -0.375 to 0.375
- l_mix: bfloat16 [256, 4096], P('feat', 'dp'), may hold values from -0.75 to 0.75
Outputs:
- grad_x: bfloat16 [16384, 2048], P('feat', 'dp')
- grad_r: float32 [64, 256, 256], P('feat', 'dp')
- grad_l: float32 [256, 4096], P('feat', 'dp')
All inputs are finite; a program needn't handle non-finite values.
Results may differ from a plain program's by a relative error of at most 0.0055.
Values may be sent and summed in bfloat16 or wider, within the bound.
No kernel may reach another device: no remote copies, remote signals or barrier semaphores. Data moves between devices by JAX's collectives and lax.ppermute only.
A program may use at most 64 MiB of HBM per device.

v0:
```python
import math
import jax
import jax.numpy as jnp
import numpy as np
from jax import lax
from jax.sharding import PartitionSpec as P

BLOCKS = 64
WIDTH = 256


def gelu_tanh(values):
    return jax.nn.gelu(values, approximate=True)


def slope_of(pre_act, upstream):
    _, pullback = jax.vjp(gelu_tanh, pre_act)
    return pullback(upstream.astype(jnp.float32))[0].astype(jnp.bfloat16)


def ring_of(mesh):
    row = mesh.devices[(slice(None),) + (0,) * (mesh.devices.ndim - 1)]
    size = len(row)
    try:
        spots = [tuple(d.coords) for d in row]
    except AttributeError:
        return list(range(size))
    near = [
        [j for j in range(size) if sum((abs(a - b) for a, b in zip(spots[i], spots[j]))) == 1]
        for i in range(size)
    ]
    path, seen, budget = ([0], {0}, [20000])

    def grow():
        budget[0] -= 1
        if budget[0] < 0:
            return False
        if len(path) == size:
            return 0 in near[path[-1]] or size <= 2
        here = path[-1]
        for nxt in sorted(near[here], key=lambda j: len([k for k in near[j] if k not in seen])):
            if nxt in seen:
                continue
            path.append(nxt)
            seen.add(nxt)
            if grow():
                return True
            path.pop()
            seen.discard(nxt)
        return False

    return list(path) if grow() else list(range(size))


def ring_reduce_scatter(parts, ring):
    n = len(ring)
    order = jnp.asarray(np.array(ring, np.int32))
    place = jnp.asarray(np.argsort(np.array(ring)).astype(np.int32))
    here = place[lax.axis_index("dp")]
    half = parts.shape[1] // 2
    halves = (parts[:, :half], parts[:, half:])
    forward = [(ring[p], ring[(p + 1) % n]) for p in range(n)]
    backward = [(ring[p], ring[(p - 1) % n]) for p in range(n)]
    totals = []
    for way, pairs, src in ((1, forward, halves[0]), (-1, backward, halves[1])):
        acc = None
        for step in range(n):
            owner = order[(here - way * (1 + step)) % n]
            mine = lax.dynamic_index_in_dim(src, owner, axis=0, keepdims=False)
            acc = mine if acc is None else acc + mine
            if step < n - 1:
                acc = lax.ppermute(acc, "dp", pairs)
        totals.append(acc)
    return jnp.concatenate(totals, axis=0)


def body(ring, activations, cotangent, r_mix, l_mix):
    tok_count = activations.shape[1]
    local_blocks = activations.shape[0] // WIDTH
    n_dp = lax.axis_size("dp")
    grad_scale = 1.0 / math.sqrt(tok_count * n_dp)
    x_blocks = activations.reshape(local_blocks, WIDTH, tok_count)
    g_blocks = cotangent.reshape(local_blocks, WIDTH, tok_count)
    g_cols = lax.all_to_all(g_blocks, "feat", split_axis=1, concat_axis=0, tiled=True)
    local_cols = l_mix.shape[0]
    rows_r = r_mix.shape[1]
    r_flat = r_mix.reshape(1, -1)
    packed = jnp.concatenate([r_flat, l_mix.reshape(1, -1)], axis=1)
    packed = lax.all_gather(packed, "dp", axis=0, tiled=True)
    r_size = r_flat.shape[1]
    r_whole = packed[:, :r_size].reshape(n_dp, local_blocks, rows_r, WIDTH)
    r_whole = jnp.transpose(r_whole, (1, 0, 2, 3)).reshape(local_blocks, n_dp * rows_r, WIDTH)
    l_whole = packed[:, r_size:].reshape(n_dp, local_cols, -1, BLOCKS)
    l_blocks = jnp.transpose(l_whole, (0, 2, 1, 3)).reshape(-1, local_cols, BLOCKS)
    mixed_rows = jnp.einsum(
        "bit,bio->bot", x_blocks, r_whole, preferred_element_type=jnp.float32
    ).astype(jnp.bfloat16)
    columns = lax.all_to_all(mixed_rows, "feat", split_axis=1, concat_axis=0, tiled=True)
    pre_act = jnp.einsum("bst,bsc->cst", columns, l_blocks, preferred_element_type=jnp.float32)
    slope_cols = slope_of(pre_act, g_cols)
    back_cols = jnp.einsum(
        "cst,bsc->sbt", slope_cols, l_blocks, preferred_element_type=jnp.float32
    ).astype(jnp.bfloat16)
    l_term = jnp.einsum("bst,cst->bsc", columns, slope_cols, preferred_element_type=jnp.float32)
    l_term = (l_term * grad_scale).reshape(n_dp, -1, local_cols, BLOCKS)
    grad_l = ring_reduce_scatter(l_term, ring)
    grad_l = jnp.transpose(grad_l, (1, 0, 2)).reshape(local_cols, -1)
    back_rows = lax.all_to_all(back_cols, "feat", split_axis=1, concat_axis=0, tiled=True)
    through_r = jnp.einsum("obt,bio->bit", back_rows, r_whole, preferred_element_type=jnp.float32)
    grad_x = (
        (g_blocks.astype(jnp.float32) + through_r)
        .astype(jnp.bfloat16)
        .reshape(local_blocks * WIDTH, tok_count)
    )
    r_term = (
        jnp.einsum("bit,obt->ibo", x_blocks, back_rows, preferred_element_type=jnp.float32)
        * grad_scale
    ).reshape(n_dp, rows_r, local_blocks, WIDTH)
    grad_r = ring_reduce_scatter(r_term, ring)
    grad_r = jnp.transpose(grad_r, (1, 0, 2))
    return (grad_x, grad_r, grad_l)


def solution(mesh):
    ring = ring_of(mesh)
    placed = (P("feat", "dp"), P("feat", "dp"), P("feat", "dp", None), P("feat", "dp"))
    return jax.shard_map(
        lambda *args: body(ring, *args),
        mesh=mesh,
        in_specs=placed,
        out_specs=(P("feat", "dp"), P("feat", "dp", None), P("feat", "dp")),
        check_vma=False,
    )
```

profile of v0, /device:TPU:0, one launch (start us, length us, event | category | flops | bytes accessed | tf_op | source)
XLA Modules:
  0.0 299.4 jit_solution(11265219353165768789)
XLA Ops:
  7.2 1.1 copy.50
  9.4 3.6 %maximum_bitcast_fusion = bf16[1,1,163840]{2,1,0:T(2,128)(2,1)} fusion(bf16[1,32768]{1,0:T(2,128)(2,1)S(1)} %bitcast.189, bf16[1,131072]{1,0:T(2,128)(2,1)S(1)} %reshape.111), kind=kLoop, calls=%fused_computation.22 | loop fusion | flops 655360 | bytes 655360
  13.0 4.1 %copy.37 = bf16[16,256,256]{2,0,1:T(8,128)(2,1)} copy(bf16[16,256,256]{2,1,0:T(8,128)(2,1)} %bitcast.183) | data formatting | bytes 4194304 | tf_op jit(solution)/shard_map/reshape | solution.py:83
  17.1 4.5 %all-to-all-start = ((bf16[16,256,256]{2,0,1:T(8,128)(2,1)}), bf16[16,256,256]{2,0,1:T(8,128)(2,1)}, u32[]{:S(2)}, u32[]{:S(2)}) async-start(bf16[16,256,256]{2,0,1:T(8,128)(2,1)} %copy.37), calls=%async_computation | async-start | bytes 4194304 | tf_op jit(solution)/shard_map/all_to_all | solution.py:84
  21.6 80.6 %all-gather.3.cloned.1.call-done = bf16[8,1,163840]{2,1,0:T(2,128)(2,1)} async-done(((bf16[1,1,163840]{2,1,0:T(2,128)(2,1)}), bf16[8,1,163840]{2,1,0:T(2,128)(2,1)}) %all-gather.3.cloned.1.call-update) | async-done | bytes 2621456 | tf_op jit(solution)/shard_map/all_gather | solution.py:89
  102.1 5.8 %copy.58 = bf16[8,1,163840]{2,0,1:T(8,128)(2,1)S(1)} copy(bf16[8,1,163840]{2,1,0:T(2,128)(2,1)} %all-gather.3.cloned.1.call-done) | data formatting | bytes 5242880
  108.1 1.4 copy-done.3
  111.5 2.5 copy.40
  114.0 4.8 %all-to-all-start.1 = ((bf16[16,256,256]{2,0,1:T(8,128)(2,1)}), bf16[16,256,256]{2,0,1:T(8,128)(2,1)}, u32[]{:S(2)}, u32[]{:S(2)}) async-start(bf16[16,256,256]{2,0,1:T(8,128)(2,1)} %copy.40), calls=%async_computation.1 | async-start | bytes 4194304 | tf_op jit(solution)/shard_map/all_to_all | solution.py:98
  160.8 4.2 %copy.38 = f32[16,4,64,256]{3,0,1,2:T(8,128)} copy(bf16[16,4,64,256]{3,0,2,1:T(8,128)(2,1)} %bitcast.92) | data formatting | bytes 6291456 | tf_op jit(solution)/shard_map/convert_element_type | solution.py:18
  166.0 2.1 reshape.115
  168.1 1.5 copy.36
  169.6 2.0 copy.41
  172.4 5.1 %fusion.6 = bf16[64,64,256]{2,0,1:T(8,128)(2,1)S(1)} fusion(f32[16,4,64,256]{3,0,1,2:T(8,128)S(1)} %copy-done.6, bf16[64,64,256]{2,0,1:T(8,128)(2,1)S(1)} %bitcast.179, bf16[64,64,64]{2,1,0:T(8,128)(2,1)S(1)} %bitcast.185), kind=kOutput, calls=%fused_computation.8 | convolution fusion | flops 155189248 | bytes 8912896 | tf_op jit(solution)/shard_map/bst,bsc->cst/dot_general | solution.py:99
  177.5 2.0 multiply_bitcast_fusion
  179.5 1.3 convolution_convert_fusion
  180.8 2.5 copy.44
  183.4 3.8 %copy.46 = f32[64,64,64]{2,1,0:T(8,128)} copy(f32[64,64,64]{0,2,1:T(8,128)} %multiply_bitcast_fusion) | data formatting | bytes 2097152 | tf_op jit(solution)/shard_map/mul | solution.py:105
  187.2 2.7 fusion.13
  189.9 4.5 %all-to-all-start.2 = ((bf16[64,64,256]{2,0,1:T(8,128)(2,1)}), bf16[64,64,256]{2,0,1:T(8,128)(2,1)}, u32[]{:S(2)}, u32[]{:S(2)}) async-start(bf16[64,64,256]{2,0,1:T(8,128)(2,1)} %copy.44), calls=%async_computation.2 | async-start | bytes 4194304 | tf_op jit(solution)/shard_map/all_to_all | solution.py:108
  195.7 1.7 collective-permute-start.14
  197.4 3.8 %collective-permute-done.21 = f32[4,64,64]{2,1,0:T(8,128)S(1)} collective-permute-done((f32[4,64,64]{2,1,0:T(8,128)S(1)}, f32[4,64,64]{2,1,0:T(8,128)S(1)}, u32[]{:S(2)}, u32[]{:S(2)}) %collective-permute-start.21) | collective-permute-done | bytes 65568 | tf_op jit(solution)/shard_map/ppermute | solution.py:72
  202.6 1.7 collective-permute-start.15
  204.3 3.1 %collective-permute-done.22 = f32[4,64,64]{2,1,0:T(8,128)S(1)} collective-permute-done((f32[4,64,64]{2,1,0:T(8,128)S(1)}, f32[4,64,64]{2,1,0:T(8,128)S(1)}, u32[]{:S(2)}, u32[]{:S(2)}) %collective-permute-start.22) | collective-permute-done | bytes 65568 | tf_op jit(solution)/shard_map/ppermute | solution.py:72
  208.7 1.7 collective-permute-start.16
  210.4 2.9 collective-permute-done.23
  214.7 1.7 collective-permute-start.17
  216.4 2.9 collective-permute-done.24
  220.6 1.7 collective-permute-start.18
  222.3 2.9 collective-permute-done.25
  226.6 1.8 copy.45
  230.5 1.7 collective-permute-start.7
  233.5 1.7 collective-permute-start.19
  235.2 2.4 collective-permute-done.7
  237.7 2.6 collective-permute-start.8
  241.4 2.1 collective-permute-start.27
  243.5 3.2 %collective-permute-done.8 = f32[16,16,256]{2,0,1:T(8,128)S(1)} collective-permute-done((f32[16,16,256]{2,0,1:T(8,128)S(1)}, f32[16,16,256]{2,0,1:T(8,128)S(1)}, u32[]{:S(2)}, u32[]{:S(2)}) %collective-permute-start.8) | collective-permute-done | bytes 262176 | tf_op jit(solution)/shard_map/ppermute | solution.py:72
  246.8 2.5 collective-permute-start.9
  249.4 1.6 collective-permute-start.20
  251.0 4.7 %collective-permute-done.9 = f32[16,16,256]{2,0,1:T(8,128)S(1)} collective-permute-done((f32[16,16,256]{2,0,1:T(8,128)S(1)}, f32[16,16,256]{2,0,1:T(8,128)S(1)}, u32[]{:S(2)}, u32[]{:S(2)}) %collective-permute-start.9) | collective-permute-done | bytes 262176 | tf_op jit(solution)/shard_map/ppermute | solution.py:72
  255.8 2.5 collective-permute-start.10
  259.4 5.3 %collective-permute-done.10 = f32[16,16,256]{2,0,1:T(8,128)S(1)} collective-permute-done((f32[16,16,256]{2,0,1:T(8,128)S(1)}, f32[16,16,256]{2,0,1:T(8,128)S(1)}, u32[]{:S(2)}, u32[]{:S(2)}) %collective-permute-start.10) | collective-permute-done | bytes 262176 | tf_op jit(solution)/shard_map/ppermute | solution.py:72
  264.7 1.7 collective-permute-start.11
  266.9 5.8 %collective-permute-done.11 = f32[16,16,256]{2,0,1:T(8,128)S(1)} collective-permute-done((f32[16,16,256]{2,0,1:T(8,128)S(1)}, f32[16,16,256]{2,0,1:T(8,128)S(1)}, u32[]{:S(2)}, u32[]{:S(2)}) %collective-permute-start.11) | collective-permute-done | bytes 262176 | tf_op jit(solution)/shard_map/ppermute | solution.py:72
  273.8 1.1 collective-permute-start.5
  275.9 4.9 %collective-permute-done.12 = f32[16,16,256]{2,0,1:T(8,128)S(1)} collective-permute-done((f32[16,16,256]{2,0,1:T(8,128)S(1)}, f32[16,16,256]{2,0,1:T(8,128)S(1)}, u32[]{:S(2)}, u32[]{:S(2)}) %collective-permute-start.12) | collective-permute-done | bytes 262176 | tf_op jit(solution)/shard_map/ppermute | solution.py:72
  283.1 1.8 collective-permute-start.6
  284.9 4.9 %add_convert_fusion = bf16[16,256,256]{2,1,0:T(8,128)(2,1)} fusion(bf16[16,256,256]{2,1,0:T(8,128)(2,1)} %bitcast.184, bf16[16,256,256]{2,1,0:T(8,128)(2,1)} %bitcast.173, bf16[256,16,256]{2,0,1:T(8,128)(2,1)} %bitcast.175), kind=kOutput, calls=%fused_computation.14 | convolution fusion | flops 540016640 | bytes 8388608 | tf_op jit(solution)/shard_map/obt,bio->bit/dot_general | solution.py:109
  (97 shorter events, 28.2 us)
Async XLA Ops:
  7.2 102.9 %copy-start = (bf16[4096,256]{1,0:T(8,128)(2,1)S(1)}, bf16[4096,256]{1,0:T(8,128)(2,1)}, u32[]{:S(2)}) copy-start(bf16[4096,256]{1,0:T(8,128)(2,1)} %param.8) | copy-start | bytes 6291460
  7.2 94.9 %all-gather.3.cloned.1.call-start = ((), (), s32[]{:S(2)}) async-start(), calls=%async_computation.3 | async-start | bytes 5898240 | tf_op jit(solution)/shard_map/all_gather | solution.py:89
  17.1 96.9 %all-to-all-start = ((bf16[16,256,256]{2,0,1:T(8,128)(2,1)}), bf16[16,256,256]{2,0,1:T(8,128)(2,1)}, u32[]{:S(2)}, u32[]{:S(2)}) async-start(bf16[16,256,256]{2,0,1:T(8,128)(2,1)} %copy.37), calls=%async_computation | async-start | bytes 4194304 | tf_op jit(solution)/shard_map/all_to_all | solution.py:84
  108.0 1.5 copy-start.3
  110.1 1.4 copy-start.1
  114.0 4.8 %copy-start.8 = (s32[8]{0:T(128)S(1)}, s32[8]{0:T(128)}, u32[]{:S(2)}) copy-start(s32[8]{0:T(128)} %constant.327.clone) | copy-start | bytes 100
  114.0 16.1 %copy-start.7 = (s32[8]{0:T(128)S(1)}, s32[8]{0:T(128)}, u32[]{:S(2)}) copy-start(s32[8]{0:T(128)} %constant.326.clone) | copy-start | bytes 100
  114.0 55.6 %all-to-all-start.1 = ((bf16[16,256,256]{2,0,1:T(8,128)(2,1)}), bf16[16,256,256]{2,0,1:T(8,128)(2,1)}, u32[]{:S(2)}, u32[]{:S(2)}) async-start(bf16[16,256,256]{2,0,1:T(8,128)(2,1)} %copy.40), calls=%async_computation.1 | async-start | bytes 4194304 | tf_op jit(solution)/shard_map/all_to_all | solution.py:98
  169.6 2.8 copy-start.6
  189.9 36.7 %all-to-all-start.2 = ((bf16[64,64,256]{2,0,1:T(8,128)(2,1)}), bf16[64,64,256]{2,0,1:T(8,128)(2,1)}, u32[]{:S(2)}, u32[]{:S(2)}) async-start(bf16[64,64,256]{2,0,1:T(8,128)(2,1)} %copy.44), calls=%async_computation.2 | async-start | bytes 4194304 | tf_op jit(solution)/shard_map/all_to_all | solution.py:108
  195.3 5.9 %collective-permute-start.21 = (f32[4,64,64]{2,1,0:T(8,128)S(1)}, f32[4,64,64]{2,1,0:T(8,128)S(1)}, u32[]{:S(2)}, u32[]{:S(2)}) collective-permute-start(f32[4,64,64]{2,1,0:T(8,128)S(1)} %dynamic-slice_bitcast_fusion.2), channel_id=1, source_target_pairs={{0,8},{4,0},{12,4},{20,12},{28,20},{24,28},{16,24},{8,16},{1,9},{5... | collective-permute-start | bytes 196616 | tf_op jit(solution)/shard_map/ppermute | solution.py:72
  195.7 6.8 %collective-permute-start.14 = (f32[4,64,64]{2,1,0:T(8,128)S(1)}, f32[4,64,64]{2,1,0:T(8,128)S(1)}, u32[]{:S(2)}, u32[]{:S(2)}) collective-permute-start(f32[4,64,64]{2,1,0:T(8,128)S(1)} %dynamic-slice_bitcast_fusion.3), channel_id=1, source_target_pairs={{0,4},{4,12},{12,20},{20,28},{28,24},{24,16},{16,8},{8,0},{1,5},{5... | collective-permute-start | bytes 196616 | tf_op jit(solution)/shard_map/ppermute | solution.py:72
  202.1 5.2 %collective-permute-start.22 = (f32[4,64,64]{2,1,0:T(8,128)S(1)}, f32[4,64,64]{2,1,0:T(8,128)S(1)}, u32[]{:S(2)}, u32[]{:S(2)}) collective-permute-start(f32[4,64,64]{2,1,0:T(8,128)S(1)} %bitcast_add_fusion.20), channel_id=1, source_target_pairs={{0,8},{4,0},{12,4},{20,12},{28,20},{24,28},{16,24},{8,16},{1,9},{5... | collective-permute-start | bytes 196616 | tf_op jit(solution)/shard_map/ppermute | solution.py:72
  202.6 6.1 %collective-permute-start.15 = (f32[4,64,64]{2,1,0:T(8,128)S(1)}, f32[4,64,64]{2,1,0:T(8,128)S(1)}, u32[]{:S(2)}, u32[]{:S(2)}) collective-permute-start(f32[4,64,64]{2,1,0:T(8,128)S(1)} %bitcast_add_fusion.27), channel_id=1, source_target_pairs={{0,4},{4,12},{12,20},{20,28},{28,24},{24,16},{16,8},{8,0},{1,5},{5... | collective-permute-start | bytes 196616 | tf_op jit(solution)/shard_map/ppermute | solution.py:72
  208.3 5.0 %collective-permute-start.23 = (f32[4,64,64]{2,1,0:T(8,128)S(1)}, f32[4,64,64]{2,1,0:T(8,128)S(1)}, u32[]{:S(2)}, u32[]{:S(2)}) collective-permute-start(f32[4,64,64]{2,1,0:T(8,128)S(1)} %bitcast_add_fusion.19), channel_id=1, source_target_pairs={{0,8},{4,0},{12,4},{20,12},{28,20},{24,28},{16,24},{8,16},{1,9},{5... | collective-permute-start | bytes 196616 | tf_op jit(solution)/shard_map/ppermute | solution.py:72
  208.7 5.9 %collective-permute-start.16 = (f32[4,64,64]{2,1,0:T(8,128)S(1)}, f32[4,64,64]{2,1,0:T(8,128)S(1)}, u32[]{:S(2)}, u32[]{:S(2)}) collective-permute-start(f32[4,64,64]{2,1,0:T(8,128)S(1)} %bitcast_add_fusion.26), channel_id=1, source_target_pairs={{0,4},{4,12},{12,20},{20,28},{28,24},{24,16},{16,8},{8,0},{1,5},{5... | collective-permute-start | bytes 196616 | tf_op jit(solution)/shard_map/ppermute | solution.py:72
  214.2 5.0 %collective-permute-start.24 = (f32[4,64,64]{2,1,0:T(8,128)S(1)}, f32[4,64,64]{2,1,0:T(8,128)S(1)}, u32[]{:S(2)}, u32[]{:S(2)}) collective-permute-start(f32[4,64,64]{2,1,0:T(8,128)S(1)} %bitcast_add_fusion.18), channel_id=1, source_target_pairs={{0,8},{4,0},{12,4},{20,12},{28,20},{24,28},{16,24},{8,16},{1,9},{5... | collective-permute-start | bytes 196616 | tf_op jit(solution)/shard_map/ppermute | solution.py:72
  214.7 5.9 %collective-permute-start.17 = (f32[4,64,64]{2,1,0:T(8,128)S(1)}, f32[4,64,64]{2,1,0:T(8,128)S(1)}, u32[]{:S(2)}, u32[]{:S(2)}) collective-permute-start(f32[4,64,64]{2,1,0:T(8,128)S(1)} %bitcast_add_fusion.25), channel_id=1, source_target_pairs={{0,4},{4,12},{12,20},{20,28},{28,24},{24,16},{16,8},{8,0},{1,5},{5... | collective-permute-start | bytes 196616 | tf_op jit(solution)/shard_map/ppermute | solution.py:72
  220.1 5.1 %collective-permute-start.25 = (f32[4,64,64]{2,1,0:T(8,128)S(1)}, f32[4,64,64]{2,1,0:T(8,128)S(1)}, u32[]{:S(2)}, u32[]{:S(2)}) collective-permute-start(f32[4,64,64]{2,1,0:T(8,128)S(1)} %bitcast_add_fusion.17), channel_id=1, source_target_pairs={{0,8},{4,0},{12,4},{20,12},{28,20},{24,28},{16,24},{8,16},{1,9},{5... | collective-permute-start | bytes 196616 | tf_op jit(solution)/shard_map/ppermute | solution.py:72
  220.6 12.0 %collective-permute-start.18 = (f32[4,64,64]{2,1,0:T(8,128)S(1)}, f32[4,64,64]{2,1,0:T(8,128)}, u32[]{:S(2)}, u32[]{:S(2)}) collective-permute-start(f32[4,64,64]{2,1,0:T(8,128)S(1)} %bitcast_add_fusion.24), channel_id=1, source_target_pairs={{0,4},{4,12},{12,20},{20,28},{28,24},{24,16},{16,8},{8,0},{1,5},{5... | collective-permute-start | bytes 196616 | tf_op jit(solution)/shard_map/ppermute | solution.py:72
  226.1 14.3 %collective-permute-start.26 = (f32[4,64,64]{2,1,0:T(8,128)S(1)}, f32[4,64,64]{2,1,0:T(8,128)S(1)}, u32[]{:S(2)}, u32[]{:S(2)}) collective-permute-start(f32[4,64,64]{2,1,0:T(8,128)S(1)} %bitcast_add_fusion.16), channel_id=1, source_target_pairs={{0,8},{4,0},{12,4},{20,12},{28,20},{24,28},{16,24},{8,16},{1,9},{5... | collective-permute-start | bytes 196616 | tf_op jit(solution)/shard_map/ppermute | solution.py:72
  228.4 1.3 copy-start.2
  230.4 42.3 %copy-start.5 = (f32[8,16,16,256]{3,1,0,2:T(8,128)}, f32[8,16,16,256]{3,1,0,2:T(8,128)S(1)}, u32[]{:S(2)}) copy-start(f32[8,16,16,256]{3,1,0,2:T(8,128)S(1)} %get-tuple-element.4) | copy-start | bytes 6291460
  230.4 43.4 %copy-start.4 = (f32[8,16,16,256]{3,1,0,2:T(8,128)}, f32[8,16,16,256]{3,1,0,2:T(8,128)S(1)}, u32[]{:S(2)}) copy-start(f32[8,16,16,256]{3,1,0,2:T(8,128)S(1)} %get-tuple-element.3) | copy-start | bytes 6291460
  230.5 7.2 %collective-permute-start.7 = (f32[16,16,256]{2,0,1:T(8,128)S(1)}, f32[16,16,256]{2,0,1:T(8,128)S(1)}, u32[]{:S(2)}, u32[]{:S(2)}) collective-permute-start(f32[16,16,256]{2,0,1:T(8,128)S(1)} %dynamic-slice_bitcast_fusion), channel_id=1, source_target_pairs={{0,8},{4,0},{12,4},{20,12},{28,20},{24,28},{16,24},{8,16},{1,9},{5... | collective-permute-start | bytes 786440 | tf_op jit(solution)/shard_map/ppermute | solution.py:72
  232.2 8.2 %collective-permute-start = (f32[16,16,256]{2,0,1:T(8,128)S(1)}, f32[16,16,256]{2,0,1:T(8,128)S(1)}, u32[]{:S(2)}, u32[]{:S(2)}) collective-permute-start(f32[16,16,256]{2,0,1:T(8,128)S(1)} %dynamic-slice_bitcast_fusion.1), channel_id=1, source_target_pairs={{0,4},{4,12},{12,20},{20,28},{28,24},{24,16},{16,8},{8,0},{1,5},{5... | collective-permute-start | bytes 786440 | tf_op jit(solution)/shard_map/ppermute | solution.py:72
  233.5 15.9 %collective-permute-start.19 = (f32[4,64,64]{2,1,0:T(8,128)S(1)}, f32[4,64,64]{2,1,0:T(8,128)S(1)}, u32[]{:S(2)}, u32[]{:S(2)}) collective-permute-start(f32[4,64,64]{2,1,0:T(8,128)S(1)} %bitcast_add_fusion.23), channel_id=1, source_target_pairs={{0,4},{4,12},{12,20},{20,28},{28,24},{24,16},{16,8},{8,0},{1,5},{5... | collective-permute-start | bytes 196616 | tf_op jit(solution)/shard_map/ppermute | solution.py:72
  237.7 9.0 %collective-permute-start.8 = (f32[16,16,256]{2,0,1:T(8,128)S(1)}, f32[16,16,256]{2,0,1:T(8,128)S(1)}, u32[]{:S(2)}, u32[]{:S(2)}) collective-permute-start(f32[16,16,256]{2,0,1:T(8,128)S(1)} %bitcast_add_fusion.6), channel_id=1, source_target_pairs={{0,8},{4,0},{12,4},{20,12},{28,20},{24,28},{16,24},{8,16},{1,9},{5... | collective-permute-start | bytes 786440 | tf_op jit(solution)/shard_map/ppermute | solution.py:72
  240.4 8.9 %collective-permute-start.1 = (f32[16,16,256]{2,0,1:T(8,128)S(1)}, f32[16,16,256]{2,0,1:T(8,128)S(1)}, u32[]{:S(2)}, u32[]{:S(2)}) collective-permute-start(f32[16,16,256]{2,0,1:T(8,128)S(1)} %bitcast_add_fusion.13), channel_id=1, source_target_pairs={{0,4},{4,12},{12,20},{20,28},{28,24},{24,16},{16,8},{8,0},{1,5},{5... | collective-permute-start | bytes 786440 | tf_op jit(solution)/shard_map/ppermute | solution.py:72
  241.4 17.0 %collective-permute-start.27 = (f32[4,64,64]{2,1,0:T(8,128)S(1)}, f32[4,64,64]{2,1,0:T(8,128)S(1)}, u32[]{:S(2)}, u32[]{:S(2)}) collective-permute-start(f32[4,64,64]{2,1,0:T(8,128)S(1)} %bitcast_add_fusion.15), channel_id=1, source_target_pairs={{0,8},{4,0},{12,4},{20,12},{28,20},{24,28},{16,24},{8,16},{1,9},{5... | collective-permute-start | bytes 196616 | tf_op jit(solution)/shard_map/ppermute | solution.py:72
  246.8 9.0 %collective-permute-start.9 = (f32[16,16,256]{2,0,1:T(8,128)S(1)}, f32[16,16,256]{2,0,1:T(8,128)S(1)}, u32[]{:S(2)}, u32[]{:S(2)}) collective-permute-start(f32[16,16,256]{2,0,1:T(8,128)S(1)} %bitcast_add_fusion.5), channel_id=1, source_target_pairs={{0,8},{4,0},{12,4},{20,12},{28,20},{24,28},{16,24},{8,16},{1,9},{5... | collective-permute-start | bytes 786440 | tf_op jit(solution)/shard_map/ppermute | solution.py:72
  249.3 9.0 %collective-permute-start.2 = (f32[16,16,256]{2,0,1:T(8,128)S(1)}, f32[16,16,256]{2,0,1:T(8,128)S(1)}, u32[]{:S(2)}, u32[]{:S(2)}) collective-permute-start(f32[16,16,256]{2,0,1:T(8,128)S(1)} %bitcast_add_fusion.12), channel_id=1, source_target_pairs={{0,4},{4,12},{12,20},{20,28},{28,24},{24,16},{16,8},{8,0},{1,5},{5... | collective-permute-start | bytes 786440 | tf_op jit(solution)/shard_map/ppermute | solution.py:72
  249.4 17.5 %collective-permute-start.20 = (f32[4,64,64]{2,1,0:T(8,128)S(1)}, f32[4,64,64]{2,1,0:T(8,128)S(1)}, u32[]{:S(2)}, u32[]{:S(2)}) collective-permute-start(f32[4,64,64]{2,1,0:T(8,128)S(1)} %bitcast_add_fusion.22), channel_id=1, source_target_pairs={{0,4},{4,12},{12,20},{20,28},{28,24},{24,16},{16,8},{8,0},{1,5},{5... | collective-permute-start | bytes 196616 | tf_op jit(solution)/shard_map/ppermute | solution.py:72
  255.8 8.9 %collective-permute-start.10 = (f32[16,16,256]{2,0,1:T(8,128)S(1)}, f32[16,16,256]{2,0,1:T(8,128)S(1)}, u32[]{:S(2)}, u32[]{:S(2)}) collective-permute-start(f32[16,16,256]{2,0,1:T(8,128)S(1)} %bitcast_add_fusion.4), channel_id=1, source_target_pairs={{0,8},{4,0},{12,4},{20,12},{28,20},{24,28},{16,24},{8,16},{1,9},{5... | collective-permute-start | bytes 786440 | tf_op jit(solution)/shard_map/ppermute | solution.py:72
  258.3 8.1 %collective-permute-start.3 = (f32[16,16,256]{2,0,1:T(8,128)S(1)}, f32[16,16,256]{2,0,1:T(8,128)S(1)}, u32[]{:S(2)}, u32[]{:S(2)}) collective-permute-start(f32[16,16,256]{2,0,1:T(8,128)S(1)} %bitcast_add_fusion.11), channel_id=1, source_target_pairs={{0,4},{4,12},{12,20},{20,28},{28,24},{24,16},{16,8},{8,0},{1,5},{5... | collective-permute-start | bytes 786440 | tf_op jit(solution)/shard_map/ppermute | solution.py:72
  264.7 8.0 %collective-permute-start.11 = (f32[16,16,256]{2,0,1:T(8,128)S(1)}, f32[16,16,256]{2,0,1:T(8,128)S(1)}, u32[]{:S(2)}, u32[]{:S(2)}) collective-permute-start(f32[16,16,256]{2,0,1:T(8,128)S(1)} %bitcast_add_fusion.3), channel_id=1, source_target_pairs={{0,8},{4,0},{12,4},{20,12},{28,20},{24,28},{16,24},{8,16},{1,9},{5... | collective-permute-start | bytes 786440 | tf_op jit(solution)/shard_map/ppermute | solution.py:72
  266.5 7.3 %collective-permute-start.4 = (f32[16,16,256]{2,0,1:T(8,128)S(1)}, f32[16,16,256]{2,0,1:T(8,128)S(1)}, u32[]{:S(2)}, u32[]{:S(2)}) collective-permute-start(f32[16,16,256]{2,0,1:T(8,128)S(1)} %bitcast_add_fusion.10), channel_id=1, source_target_pairs={{0,4},{4,12},{12,20},{20,28},{28,24},{24,16},{16,8},{8,0},{1,5},{5... | collective-permute-start | bytes 786440 | tf_op jit(solution)/shard_map/ppermute | solution.py:72
  272.7 8.0 %collective-permute-start.12 = (f32[16,16,256]{2,0,1:T(8,128)S(1)}, f32[16,16,256]{2,0,1:T(8,128)S(1)}, u32[]{:S(2)}, u32[]{:S(2)}) collective-permute-start(f32[16,16,256]{2,0,1:T(8,128)S(1)} %bitcast_add_fusion.2), channel_id=1, source_target_pairs={{0,8},{4,0},{12,4},{20,12},{28,20},{24,28},{16,24},{8,16},{1,9},{5... | collective-permute-start | bytes 786440 | tf_op jit(solution)/shard_map/ppermute | solution.py:72
  273.8 8.3 %collective-permute-start.5 = (f32[16,16,256]{2,0,1:T(8,128)S(1)}, f32[16,16,256]{2,0,1:T(8,128)S(1)}, u32[]{:S(2)}, u32[]{:S(2)}) collective-permute-start(f32[16,16,256]{2,0,1:T(8,128)S(1)} %bitcast_add_fusion.9), channel_id=1, source_target_pairs={{0,4},{4,12},{12,20},{20,28},{28,24},{24,16},{16,8},{8,0},{1,5},{5... | collective-permute-start | bytes 786440 | tf_op jit(solution)/shard_map/ppermute | solution.py:72
  281.7 8.0 %collective-permute-start.13 = (f32[16,16,256]{2,0,1:T(8,128)S(1)}, f32[16,16,256]{2,0,1:T(8,128)S(1)}, u32[]{:S(2)}, u32[]{:S(2)}) collective-permute-start(f32[16,16,256]{2,0,1:T(8,128)S(1)} %bitcast_add_fusion.1), channel_id=1, source_target_pairs={{0,8},{4,0},{12,4},{20,12},{28,20},{24,28},{16,24},{8,16},{1,9},{5... | collective-permute-start | bytes 786440 | tf_op jit(solution)/shard_map/ppermute | solution.py:72
  283.1 7.7 %collective-permute-start.6 = (f32[16,16,256]{2,0,1:T(8,128)S(1)}, f32[16,16,256]{2,0,1:T(8,128)S(1)}, u32[]{:S(2)}, u32[]{:S(2)}) collective-permute-start(f32[16,16,256]{2,0,1:T(8,128)S(1)} %bitcast_add_fusion.8), channel_id=1, source_target_pairs={{0,4},{4,12},{12,20},{20,28},{28,24},{24,16},{16,8},{8,0},{1,5},{5... | collective-permute-start | bytes 786440 | tf_op jit(solution)/shard_map/ppermute | solution.py:72
Sparse Core Ops, SparseCore 0:
  13.1 88.9 all-gather.2
where the time goes:
time: 301 us; the launch traced here: 299 us
  waiting for transfers between devices  122 us (41%)
  between operations  55.1 us (18%)
  starting transfers between devices  46.6 us (15%)
  local copies, waits for them, and re-layouts  44.2 us (15%)
  other arithmetic  16.3 us (5%)
  matrix products  14.8 us (5%)
    all_gather x1, waiting for transfers between devices, body(): packed = lax.all_gather(packed, 'dp', axis=0, tiled=True)  80.6 us
    ppermute x28, waiting for transfers between devices, ring_reduce_scatter(): acc = lax.ppermute(acc, 'dp', pairs)  41.8 us
    ppermute x28, starting transfers between devices, ring_reduce_scatter(): acc = lax.ppermute(acc, 'dp', pairs)  32.9 us
    add x28, other arithmetic, ring_reduce_scatter(): acc = mine if acc is None else acc + mine  11.8 us
    unnamed x20, local copies, waits for them, and re-layouts  10.3 us
  transfers between devices with their start and end apart: 32, of which 13 were waited for; matrix products, arithmetic and copies ran while one was open for 15% of the time, Pallas kernels for 0%

commit v1 on v0

--- a/solution.py
+++ b/solution.py
@@ -75,6 +75,15 @@
 
 
 def body(ring, activations, cotangent, r_mix, l_mix):
+
+    def frames_pair(chunk):
+        u_next = lax.axis_size("feat")
+        y_new = jnp.split(chunk, u_next, axis=1)
+        shaped = jnp.stack(y_new)
+        main = lax.all_to_all(shaped, "feat", split_axis=0, concat_axis=0)
+        wide_out = jnp.concatenate(main, axis=0)
+        return wide_out
+
     tok_count = activations.shape[1]
     local_blocks = activations.shape[0] // WIDTH
     n_dp = lax.axis_size("dp")
@@ -95,7 +104,7 @@
     mixed_rows = jnp.einsum(
         "bit,bio->bot", x_blocks, r_whole, preferred_element_type=jnp.float32
     ).astype(jnp.bfloat16)
-    columns = lax.all_to_all(mixed_rows, "feat", split_axis=1, concat_axis=0, tiled=True)
+    columns = frames_pair(mixed_rows)
     pre_act = jnp.einsum("bst,bsc->cst", columns, l_blocks, preferred_element_type=jnp.float32)
     slope_cols = slope_of(pre_act, g_cols)
     back_cols = jnp.einsum(

time: 301 us -> 302 us (level)
  local copies, waits for them, and re-layouts: 44.2 us -> 39.1 us
  matrix products: 14.8 us -> 19.2 us
    unnamed x20 -> x18, local copies, waits for them, and re-layouts: 10.3 us -> 9.49 us
where the time goes in v1:
time: 302 us; the launch traced here: 300 us
  waiting for transfers between devices  123 us (41%)
  between operations  55 us (18%)
  starting transfers between devices  46.6 us (15%)
  local copies, waits for them, and re-layouts  39.1 us (13%)
  matrix products  19.2 us (6%)
  other arithmetic  17.9 us (6%)
    all_gather x1, waiting for transfers between devices, body(): packed = lax.all_gather(packed, 'dp', axis=0, tiled=True)  80.6 us
    ppermute x28, waiting for transfers between devices, ring_reduce_scatter(): acc = lax.ppermute(acc, 'dp', pairs)  42 us
    ppermute x28, starting transfers between devices, ring_reduce_scatter(): acc = lax.ppermute(acc, 'dp', pairs)  32.9 us
    add x28, other arithmetic, ring_reduce_scatter(): acc = mine if acc is None else acc + mine  11.8 us
    unnamed x18, local copies, waits for them, and re-layouts  9.49 us
    dot_general x1, matrix products, body(): jnp.einsum('bst,bsc->cst', columns, l_blocks, preferred_element_type=jnp....  7 us
  transfers between devices with their start and end apart: 32, of which 13 were waited for; matrix products, arithmetic and copies ran while one was open for 15% of the time, Pallas kernels for 0%

profile of v1, /device:TPU:0, one launch (start us, length us, event | category | flops | bytes accessed | tf_op | source)
XLA Modules:
  0.0 300.3 jit_solution(3507732845981775973)
XLA Ops:
  7.2 1.1 copy.53
  9.4 3.6 %maximum_bitcast_fusion = bf16[1,1,163840]{2,1,0:T(2,128)(2,1)} fusion(bf16[1,32768]{1,0:T(2,128)(2,1)S(1)} %bitcast.190, bf16[1,131072]{1,0:T(2,128)(2,1)S(1)} %reshape.114), kind=kLoop, calls=%fused_computation.26 | loop fusion | flops 655360 | bytes 655360
  13.0 4.1 %copy.40 = bf16[16,256,256]{2,0,1:T(8,128)(2,1)} copy(bf16[16,256,256]{2,1,0:T(8,128)(2,1)} %bitcast.184) | data formatting | bytes 4194304 | tf_op jit(solution)/shard_map/reshape | solution.py:92
  17.1 4.5 %all-to-all-start = ((bf16[16,256,256]{2,0,1:T(8,128)(2,1)}), bf16[16,256,256]{2,0,1:T(8,128)(2,1)}, u32[]{:S(2)}, u32[]{:S(2)}) async-start(bf16[16,256,256]{2,0,1:T(8,128)(2,1)} %copy.40), calls=%async_computation | async-start | bytes 4194304 | tf_op jit(solution)/shard_map/all_to_all | solution.py:93
  21.6 80.6 %all-gather.3.cloned.1.call-done = bf16[8,1,163840]{2,1,0:T(2,128)(2,1)} async-done(((bf16[1,1,163840]{2,1,0:T(2,128)(2,1)}), bf16[8,1,163840]{2,1,0:T(2,128)(2,1)}) %all-gather.3.cloned.1.call-update) | async-done | bytes 2621456 | tf_op jit(solution)/shard_map/all_gather | solution.py:98
  102.1 5.8 %copy.67 = bf16[8,1,163840]{2,0,1:T(8,128)(2,1)S(1)} copy(bf16[8,1,163840]{2,1,0:T(2,128)(2,1)} %all-gather.3.cloned.1.call-done) | data formatting | bytes 5242880
  108.1 1.4 copy-done.3
  111.6 1.6 pad_maximum_fusion
  113.2 4.8 %all-to-all-start.1 = ((bf16[4,16,64,256]{3,2,1,0:T(8,128)(2,1)}), bf16[4,16,64,256]{3,2,1,0:T(8,128)(2,1)}, u32[]{:S(2)}, u32[]{:S(2)}) async-start(bf16[4,16,64,256]{3,2,1,0:T(8,128)(2,1)} %pad_maximum_fusion), calls=%async_computation.1 | async-start | bytes 4194304 | tf_op jit(solution)/shard_map/all_to_all | solution.py:83
  160.0 4.2 %copy.41 = f32[16,4,64,256]{3,0,1,2:T(8,128)} copy(bf16[16,4,64,256]{3,0,2,1:T(8,128)(2,1)} %bitcast.93) | data formatting | bytes 6291456 | tf_op jit(solution)/shard_map/convert_element_type | solution.py:18
  164.1 1.1 slice.25
  165.2 2.1 reshape.118
  167.3 1.5 copy.39
  168.8 7.0 %fusion.6 = bf16[64,64,256]{2,0,1:T(8,128)(2,1)S(1)} fusion(f32[16,4,64,256]{3,0,1,2:T(8,128)} %copy.41, bf16[64,64,256]{2,1,0:T(8,128)(2,1)} %bitcast.14, bf16[64,64,64]{2,1,0:T(8,128)(2,1)S(1)} %bitcast.186), kind=kOutput, calls=%fused_computation.8 | convolution fusion | flops 155189248 | bytes 8912896 | tf_op jit(solution)/shard_map/bst,bsc->cst/dot_general | solution.py:108
  175.8 4.5 %multiply_bitcast_fusion = f32[64,64,64]{0,2,1:T(8,128)} fusion(bf16[64,64,256]{2,0,1:T(8,128)(2,1)S(1)} %fusion.6, bf16[64,64,256]{2,1,0:T(8,128)(2,1)} %bitcast.14), kind=kOutput, calls=%fused_computation.18 | convolution fusion | flops 134479872 | bytes 5242880 | tf_op jit(solution)/shard_map/bst,cst->bsc/dot_general | solution.py:113
  180.3 1.3 convolution_convert_fusion
  181.6 2.5 copy.46
  184.1 3.8 %copy.49 = f32[64,64,64]{2,1,0:T(8,128)} copy(f32[64,64,64]{0,2,1:T(8,128)} %multiply_bitcast_fusion) | data formatting | bytes 2097152 | tf_op jit(solution)/shard_map/mul | solution.py:114
  187.9 2.7 fusion.18
  190.6 4.5 %all-to-all-start.2 = ((bf16[64,64,256]{2,0,1:T(8,128)(2,1)}), bf16[64,64,256]{2,0,1:T(8,128)(2,1)}, u32[]{:S(2)}, u32[]{:S(2)}) async-start(bf16[64,64,256]{2,0,1:T(8,128)(2,1)} %copy.46), calls=%async_computation.2 | async-start | bytes 4194304 | tf_op jit(solution)/shard_map/all_to_all | solution.py:117
  196.5 1.7 collective-permute-start.14
  198.2 3.8 %collective-permute-done.21 = f32[4,64,64]{2,1,0:T(8,128)S(1)} collective-permute-done((f32[4,64,64]{2,1,0:T(8,128)S(1)}, f32[4,64,64]{2,1,0:T(8,128)S(1)}, u32[]{:S(2)}, u32[]{:S(2)}) %collective-permute-start.21) | collective-permute-done | bytes 65568 | tf_op jit(solution)/shard_map/ppermute | solution.py:72
  203.3 1.7 collective-permute-start.15
  205.0 3.1 %collective-permute-done.22 = f32[4,64,64]{2,1,0:T(8,128)S(1)} collective-permute-done((f32[4,64,64]{2,1,0:T(8,128)S(1)}, f32[4,64,64]{2,1,0:T(8,128)S(1)}, u32[]{:S(2)}, u32[]{:S(2)}) %collective-permute-start.22) | collective-permute-done | bytes 65568 | tf_op jit(solution)/shard_map/ppermute | solution.py:72
  209.5 1.7 collective-permute-start.16
  211.2 2.9 collective-permute-done.23
  215.7 1.7 collective-permute-start.17
  217.3 2.9 collective-permute-done.24
  221.6 1.7 collective-permute-start.18
  223.3 2.9 collective-permute-done.25
  227.6 1.8 copy.47
  231.4 1.7 collective-permute-start.7
  234.5 1.7 collective-permute-start.19
  236.2 2.6 collective-permute-done.7
  238.9 2.4 collective-permute-start.8
  242.6 2.1 collective-permute-start.27
  244.7 3.1 %collective-permute-done.8 = f32[16,16,256]{2,0,1:T(8,128)S(1)} collective-permute-done((f32[16,16,256]{2,0,1:T(8,128)S(1)}, f32[16,16,256]{2,0,1:T(8,128)S(1)}, u32[]{:S(2)}, u32[]{:S(2)}) %collective-permute-start.8) | collective-permute-done | bytes 262176 | tf_op jit(solution)/shard_map/ppermute | solution.py:72
  247.8 2.5 collective-permute-start.9
  250.5 1.6 collective-permute-start.20
  252.1 4.6 %collective-permute-done.9 = f32[16,16,256]{2,0,1:T(8,128)S(1)} collective-permute-done((f32[16,16,256]{2,0,1:T(8,128)S(1)}, f32[16,16,256]{2,0,1:T(8,128)S(1)}, u32[]{:S(2)}, u32[]{:S(2)}) %collective-permute-start.9) | collective-permute-done | bytes 262176 | tf_op jit(solution)/shard_map/ppermute | solution.py:72
  256.8 2.5 collective-permute-start.10
  260.4 5.4 %collective-permute-done.10 = f32[16,16,256]{2,0,1:T(8,128)S(1)} collective-permute-done((f32[16,16,256]{2,0,1:T(8,128)S(1)}, f32[16,16,256]{2,0,1:T(8,128)S(1)}, u32[]{:S(2)}, u32[]{:S(2)}) %collective-permute-start.10) | collective-permute-done | bytes 262176 | tf_op jit(solution)/shard_map/ppermute | solution.py:72
  265.8 1.6 collective-permute-start.11
  268.0 5.7 %collective-permute-done.11 = f32[16,16,256]{2,0,1:T(8,128)S(1)} collective-permute-done((f32[16,16,256]{2,0,1:T(8,128)S(1)}, f32[16,16,256]{2,0,1:T(8,128)S(1)}, u32[]{:S(2)}, u32[]{:S(2)}) %collective-permute-start.11) | collective-permute-done | bytes 262176 | tf_op jit(solution)/shard_map/ppermute | solution.py:72
  274.7 1.2 collective-permute-start.5
  276.8 4.8 %collective-permute-done.12 = f32[16,16,256]{2,0,1:T(8,128)S(1)} collective-permute-done((f32[16,16,256]{2,0,1:T(8,128)S(1)}, f32[16,16,256]{2,0,1:T(8,128)S(1)}, u32[]{:S(2)}, u32[]{:S(2)}) %collective-permute-start.12) | collective-permute-done | bytes 262176 | tf_op jit(solution)/shard_map/ppermute | solution.py:72
  284.0 1.8 collective-permute-start.6
  285.8 4.9 %add_convert_fusion = bf16[16,256,256]{2,1,0:T(8,128)(2,1)} fusion(bf16[16,256,256]{2,1,0:T(8,128)(2,1)} %bitcast.185, bf16[16,256,256]{2,1,0:T(8,128)(2,1)} %bitcast.176, bf16[256,16,256]{2,0,1:T(8,128)(2,1)} %bitcast.178), kind=kOutput, calls=%fused_computation.14 | convolution fusion | flops 540016640 | bytes 8388608 | tf_op jit(solution)/shard_map/obt,bio->bit/dot_general | solution.py:118
  (95 shorter events, 26.9 us)
Async XLA Ops:
  7.2 102.9 %copy-start = (bf16[4096,256]{1,0:T(8,128)(2,1)S(1)}, bf16[4096,256]{1,0:T(8,128)(2,1)}, u32[]{:S(2)}) copy-start(bf16[4096,256]{1,0:T(8,128)(2,1)} %param.8) | copy-start | bytes 6291460
  7.2 94.9 %all-gather.3.cloned.1.call-start = ((), (), s32[]{:S(2)}) async-start(), calls=%async_computation.3 | async-start | bytes 5898240 | tf_op jit(solution)/shard_map/all_gather | solution.py:98
  17.1 96.1 %all-to-all-start = ((bf16[16,256,256]{2,0,1:T(8,128)(2,1)}), bf16[16,256,256]{2,0,1:T(8,128)(2,1)}, u32[]{:S(2)}, u32[]{:S(2)}) async-start(bf16[16,256,256]{2,0,1:T(8,128)(2,1)} %copy.40), calls=%async_computation | async-start | bytes 4194304 | tf_op jit(solution)/shard_map/all_to_all | solution.py:93
  108.0 1.5 copy-start.3
  110.1 1.4 copy-start.1
  113.2 4.8 %copy-start.7 = (s32[8]{0:T(128)S(1)}, s32[8]{0:T(128)}, u32[]{:S(2)}) copy-start(s32[8]{0:T(128)} %constant.327.clone) | copy-start | bytes 100
  113.2 16.1 %copy-start.6 = (s32[8]{0:T(128)S(1)}, s32[8]{0:T(128)}, u32[]{:S(2)}) copy-start(s32[8]{0:T(128)} %constant.326.clone) | copy-start | bytes 100
  113.2 55.6 %all-to-all-start.1 = ((bf16[4,16,64,256]{3,2,1,0:T(8,128)(2,1)}), bf16[4,16,64,256]{3,2,1,0:T(8,128)(2,1)}, u32[]{:S(2)}, u32[]{:S(2)}) async-start(bf16[4,16,64,256]{3,2,1,0:T(8,128)(2,1)} %pad_maximum_fusion), calls=%async_computation.1 | async-start | bytes 4194304 | tf_op jit(solution)/shard_map/all_to_all | solution.py:83
  190.6 36.9 %all-to-all-start.2 = ((bf16[64,64,256]{2,0,1:T(8,128)(2,1)}), bf16[64,64,256]{2,0,1:T(8,128)(2,1)}, u32[]{:S(2)}, u32[]{:S(2)}) async-start(bf16[64,64,256]{2,0,1:T(8,128)(2,1)} %copy.46), calls=%async_computation.2 | async-start | bytes 4194304 | tf_op jit(solution)/shard_map/all_to_all | solution.py:117
  196.0 5.9 %collective-permute-start.21 = (f32[4,64,64]{2,1,0:T(8,128)S(1)}, f32[4,64,64]{2,1,0:T(8,128)S(1)}, u32[]{:S(2)}, u32[]{:S(2)}) collective-permute-start(f32[4,64,64]{2,1,0:T(8,128)S(1)} %dynamic-slice_bitcast_fusion.2), channel_id=1, source_target_pairs={{0,8},{4,0},{12,4},{20,12},{28,20},{24,28},{16,24},{8,16},{1,9},{5... | collective-permute-start | bytes 196616 | tf_op jit(solution)/shard_map/ppermute | solution.py:72
  196.5 6.8 %collective-permute-start.14 = (f32[4,64,64]{2,1,0:T(8,128)S(1)}, f32[4,64,64]{2,1,0:T(8,128)S(1)}, u32[]{:S(2)}, u32[]{:S(2)}) collective-permute-start(f32[4,64,64]{2,1,0:T(8,128)S(1)} %dynamic-slice_bitcast_fusion.3), channel_id=1, source_target_pairs={{0,4},{4,12},{12,20},{20,28},{28,24},{24,16},{16,8},{8,0},{1,5},{5... | collective-permute-start | bytes 196616 | tf_op jit(solution)/shard_map/ppermute | solution.py:72
  202.9 5.2 %collective-permute-start.22 = (f32[4,64,64]{2,1,0:T(8,128)S(1)}, f32[4,64,64]{2,1,0:T(8,128)S(1)}, u32[]{:S(2)}, u32[]{:S(2)}) collective-permute-start(f32[4,64,64]{2,1,0:T(8,128)S(1)} %bitcast_add_fusion.20), channel_id=1, source_target_pairs={{0,8},{4,0},{12,4},{20,12},{28,20},{24,28},{16,24},{8,16},{1,9},{5... | collective-permute-start | bytes 196616 | tf_op jit(solution)/shard_map/ppermute | solution.py:72
  203.3 6.1 %collective-permute-start.15 = (f32[4,64,64]{2,1,0:T(8,128)S(1)}, f32[4,64,64]{2,1,0:T(8,128)S(1)}, u32[]{:S(2)}, u32[]{:S(2)}) collective-permute-start(f32[4,64,64]{2,1,0:T(8,128)S(1)} %bitcast_add_fusion.27), channel_id=1, source_target_pairs={{0,4},{4,12},{12,20},{20,28},{28,24},{24,16},{16,8},{8,0},{1,5},{5... | collective-permute-start | bytes 196616 | tf_op jit(solution)/shard_map/ppermute | solution.py:72
  209.0 5.0 %collective-permute-start.23 = (f32[4,64,64]{2,1,0:T(8,128)S(1)}, f32[4,64,64]{2,1,0:T(8,128)S(1)}, u32[]{:S(2)}, u32[]{:S(2)}) collective-permute-start(f32[4,64,64]{2,1,0:T(8,128)S(1)} %bitcast_add_fusion.19), channel_id=1, source_target_pairs={{0,8},{4,0},{12,4},{20,12},{28,20},{24,28},{16,24},{8,16},{1,9},{5... | collective-permute-start | bytes 196616 | tf_op jit(solution)/shard_map/ppermute | solution.py:72
  209.5 6.1 %collective-permute-start.16 = (f32[4,64,64]{2,1,0:T(8,128)S(1)}, f32[4,64,64]{2,1,0:T(8,128)S(1)}, u32[]{:S(2)}, u32[]{:S(2)}) collective-permute-start(f32[4,64,64]{2,1,0:T(8,128)S(1)} %bitcast_add_fusion.26), channel_id=1, source_target_pairs={{0,4},{4,12},{12,20},{20,28},{28,24},{24,16},{16,8},{8,0},{1,5},{5... | collective-permute-start | bytes 196616 | tf_op jit(solution)/shard_map/ppermute | solution.py:72
  215.0 5.2 %collective-permute-start.24 = (f32[4,64,64]{2,1,0:T(8,128)S(1)}, f32[4,64,64]{2,1,0:T(8,128)S(1)}, u32[]{:S(2)}, u32[]{:S(2)}) collective-permute-start(f32[4,64,64]{2,1,0:T(8,128)S(1)} %bitcast_add_fusion.18), channel_id=1, source_target_pairs={{0,8},{4,0},{12,4},{20,12},{28,20},{24,28},{16,24},{8,16},{1,9},{5... | collective-permute-start | bytes 196616 | tf_op jit(solution)/shard_map/ppermute | solution.py:72
  215.7 5.9 %collective-permute-start.17 = (f32[4,64,64]{2,1,0:T(8,128)S(1)}, f32[4,64,64]{2,1,0:T(8,128)S(1)}, u32[]{:S(2)}, u32[]{:S(2)}) collective-permute-start(f32[4,64,64]{2,1,0:T(8,128)S(1)} %bitcast_add_fusion.25), channel_id=1, source_target_pairs={{0,4},{4,12},{12,20},{20,28},{28,24},{24,16},{16,8},{8,0},{1,5},{5... | collective-permute-start | bytes 196616 | tf_op jit(solution)/shard_map/ppermute | solution.py:72
  221.1 5.1 %collective-permute-start.25 = (f32[4,64,64]{2,1,0:T(8,128)S(1)}, f32[4,64,64]{2,1,0:T(8,128)S(1)}, u32[]{:S(2)}, u32[]{:S(2)}) collective-permute-start(f32[4,64,64]{2,1,0:T(8,128)S(1)} %bitcast_add_fusion.17), channel_id=1, source_target_pairs={{0,8},{4,0},{12,4},{20,12},{28,20},{24,28},{16,24},{8,16},{1,9},{5... | collective-permute-start | bytes 196616 | tf_op jit(solution)/shard_map/ppermute | solution.py:72
  221.6 12.0 %collective-permute-start.18 = (f32[4,64,64]{2,1,0:T(8,128)S(1)}, f32[4,64,64]{2,1,0:T(8,128)}, u32[]{:S(2)}, u32[]{:S(2)}) collective-permute-start(f32[4,64,64]{2,1,0:T(8,128)S(1)} %bitcast_add_fusion.24), channel_id=1, source_target_pairs={{0,4},{4,12},{12,20},{20,28},{28,24},{24,16},{16,8},{8,0},{1,5},{5... | collective-permute-start | bytes 196616 | tf_op jit(solution)/shard_map/ppermute | solution.py:72
  227.1 14.6 %collective-permute-start.26 = (f32[4,64,64]{2,1,0:T(8,128)S(1)}, f32[4,64,64]{2,1,0:T(8,128)S(1)}, u32[]{:S(2)}, u32[]{:S(2)}) collective-permute-start(f32[4,64,64]{2,1,0:T(8,128)S(1)} %bitcast_add_fusion.16), channel_id=1, source_target_pairs={{0,8},{4,0},{12,4},{20,12},{28,20},{24,28},{16,24},{8,16},{1,9},{5... | collective-permute-start | bytes 196616 | tf_op jit(solution)/shard_map/ppermute | solution.py:72
  229.4 1.3 copy-start.2
  231.4 42.3 %copy-start.5 = (f32[8,16,16,256]{3,1,0,2:T(8,128)}, f32[8,16,16,256]{3,1,0,2:T(8,128)S(1)}, u32[]{:S(2)}) copy-start(f32[8,16,16,256]{3,1,0,2:T(8,128)S(1)} %get-tuple-element.4) | copy-start | bytes 6291460
  231.4 43.2 %copy-start.4 = (f32[8,16,16,256]{3,1,0,2:T(8,128)}, f32[8,16,16,256]{3,1,0,2:T(8,128)S(1)}, u32[]{:S(2)}) copy-start(f32[8,16,16,256]{3,1,0,2:T(8,128)S(1)} %get-tuple-element.3) | copy-start | bytes 6291460
  231.4 7.4 %collective-permute-start.7 = (f32[16,16,256]{2,0,1:T(8,128)S(1)}, f32[16,16,256]{2,0,1:T(8,128)S(1)}, u32[]{:S(2)}, u32[]{:S(2)}) collective-permute-start(f32[16,16,256]{2,0,1:T(8,128)S(1)} %dynamic-slice_bitcast_fusion), channel_id=1, source_target_pairs={{0,8},{4,0},{12,4},{20,12},{28,20},{24,28},{16,24},{8,16},{1,9},{5... | collective-permute-start | bytes 786440 | tf_op jit(solution)/shard_map/ppermute | solution.py:72
  233.2 8.4 %collective-permute-start = (f32[16,16,256]{2,0,1:T(8,128)S(1)}, f32[16,16,256]{2,0,1:T(8,128)S(1)}, u32[]{:S(2)}, u32[]{:S(2)}) collective-permute-start(f32[16,16,256]{2,0,1:T(8,128)S(1)} %dynamic-slice_bitcast_fusion.1), channel_id=1, source_target_pairs={{0,4},{4,12},{12,20},{20,28},{28,24},{24,16},{16,8},{8,0},{1,5},{5... | collective-permute-start | bytes 786440 | tf_op jit(solution)/shard_map/ppermute | solution.py:72
  234.5 15.9 %collective-permute-start.19 = (f32[4,64,64]{2,1,0:T(8,128)S(1)}, f32[4,64,64]{2,1,0:T(8,128)S(1)}, u32[]{:S(2)}, u32[]{:S(2)}) collective-permute-start(f32[4,64,64]{2,1,0:T(8,128)S(1)} %bitcast_add_fusion.23), channel_id=1, source_target_pairs={{0,4},{4,12},{12,20},{20,28},{28,24},{24,16},{16,8},{8,0},{1,5},{5... | collective-permute-start | bytes 196616 | tf_op jit(solution)/shard_map/ppermute | solution.py:72
  238.9 8.9 %collective-permute-start.8 = (f32[16,16,256]{2,0,1:T(8,128)S(1)}, f32[16,16,256]{2,0,1:T(8,128)S(1)}, u32[]{:S(2)}, u32[]{:S(2)}) collective-permute-start(f32[16,16,256]{2,0,1:T(8,128)S(1)} %bitcast_add_fusion.6), channel_id=1, source_target_pairs={{0,8},{4,0},{12,4},{20,12},{28,20},{24,28},{16,24},{8,16},{1,9},{5... | collective-permute-start | bytes 786440 | tf_op jit(solution)/shard_map/ppermute | solution.py:72
  241.6 8.7 %collective-permute-start.1 = (f32[16,16,256]{2,0,1:T(8,128)S(1)}, f32[16,16,256]{2,0,1:T(8,128)S(1)}, u32[]{:S(2)}, u32[]{:S(2)}) collective-permute-start(f32[16,16,256]{2,0,1:T(8,128)S(1)} %bitcast_add_fusion.13), channel_id=1, source_target_pairs={{0,4},{4,12},{12,20},{20,28},{28,24},{24,16},{16,8},{8,0},{1,5},{5... | collective-permute-start | bytes 786440 | tf_op jit(solution)/shard_map/ppermute | solution.py:72
  242.6 16.8 %collective-permute-start.27 = (f32[4,64,64]{2,1,0:T(8,128)S(1)}, f32[4,64,64]{2,1,0:T(8,128)S(1)}, u32[]{:S(2)}, u32[]{:S(2)}) collective-permute-start(f32[4,64,64]{2,1,0:T(8,128)S(1)} %bitcast_add_fusion.15), channel_id=1, source_target_pairs={{0,8},{4,0},{12,4},{20,12},{28,20},{24,28},{16,24},{8,16},{1,9},{5... | collective-permute-start | bytes 196616 | tf_op jit(solution)/shard_map/ppermute | solution.py:72
  247.8 8.9 %collective-permute-start.9 = (f32[16,16,256]{2,0,1:T(8,128)S(1)}, f32[16,16,256]{2,0,1:T(8,128)S(1)}, u32[]{:S(2)}, u32[]{:S(2)}) collective-permute-start(f32[16,16,256]{2,0,1:T(8,128)S(1)} %bitcast_add_fusion.5), channel_id=1, source_target_pairs={{0,8},{4,0},{12,4},{20,12},{28,20},{24,28},{16,24},{8,16},{1,9},{5... | collective-permute-start | bytes 786440 | tf_op jit(solution)/shard_map/ppermute | solution.py:72
  250.4 8.9 %collective-permute-start.2 = (f32[16,16,256]{2,0,1:T(8,128)S(1)}, f32[16,16,256]{2,0,1:T(8,128)S(1)}, u32[]{:S(2)}, u32[]{:S(2)}) collective-permute-start(f32[16,16,256]{2,0,1:T(8,128)S(1)} %bitcast_add_fusion.12), channel_id=1, source_target_pairs={{0,4},{4,12},{12,20},{20,28},{28,24},{24,16},{16,8},{8,0},{1,5},{5... | collective-permute-start | bytes 786440 | tf_op jit(solution)/shard_map/ppermute | solution.py:72
  250.5 17.5 %collective-permute-start.20 = (f32[4,64,64]{2,1,0:T(8,128)S(1)}, f32[4,64,64]{2,1,0:T(8,128)S(1)}, u32[]{:S(2)}, u32[]{:S(2)}) collective-permute-start(f32[4,64,64]{2,1,0:T(8,128)S(1)} %bitcast_add_fusion.22), channel_id=1, source_target_pairs={{0,4},{4,12},{12,20},{20,28},{28,24},{24,16},{16,8},{8,0},{1,5},{5... | collective-permute-start | bytes 196616 | tf_op jit(solution)/shard_map/ppermute | solution.py:72
  256.8 9.0 %collective-permute-start.10 = (f32[16,16,256]{2,0,1:T(8,128)S(1)}, f32[16,16,256]{2,0,1:T(8,128)S(1)}, u32[]{:S(2)}, u32[]{:S(2)}) collective-permute-start(f32[16,16,256]{2,0,1:T(8,128)S(1)} %bitcast_add_fusion.4), channel_id=1, source_target_pairs={{0,8},{4,0},{12,4},{20,12},{28,20},{24,28},{16,24},{8,16},{1,9},{5... | collective-permute-start | bytes 786440 | tf_op jit(solution)/shard_map/ppermute | solution.py:72
  259.3 8.1 %collective-permute-start.3 = (f32[16,16,256]{2,0,1:T(8,128)S(1)}, f32[16,16,256]{2,0,1:T(8,128)S(1)}, u32[]{:S(2)}, u32[]{:S(2)}) collective-permute-start(f32[16,16,256]{2,0,1:T(8,128)S(1)} %bitcast_add_fusion.11), channel_id=1, source_target_pairs={{0,4},{4,12},{12,20},{20,28},{28,24},{24,16},{16,8},{8,0},{1,5},{5... | collective-permute-start | bytes 786440 | tf_op jit(solution)/shard_map/ppermute | solution.py:72
  265.8 7.9 %collective-permute-start.11 = (f32[16,16,256]{2,0,1:T(8,128)S(1)}, f32[16,16,256]{2,0,1:T(8,128)S(1)}, u32[]{:S(2)}, u32[]{:S(2)}) collective-permute-start(f32[16,16,256]{2,0,1:T(8,128)S(1)} %bitcast_add_fusion.3), channel_id=1, source_target_pairs={{0,8},{4,0},{12,4},{20,12},{28,20},{24,28},{16,24},{8,16},{1,9},{5... | collective-permute-start | bytes 786440 | tf_op jit(solution)/shard_map/ppermute | solution.py:72
  267.4 7.2 %collective-permute-start.4 = (f32[16,16,256]{2,0,1:T(8,128)S(1)}, f32[16,16,256]{2,0,1:T(8,128)S(1)}, u32[]{:S(2)}, u32[]{:S(2)}) collective-permute-start(f32[16,16,256]{2,0,1:T(8,128)S(1)} %bitcast_add_fusion.10), channel_id=1, source_target_pairs={{0,4},{4,12},{12,20},{20,28},{28,24},{24,16},{16,8},{8,0},{1,5},{5... | collective-permute-start | bytes 786440 | tf_op jit(solution)/shard_map/ppermute | solution.py:72
  273.7 7.9 %collective-permute-start.12 = (f32[16,16,256]{2,0,1:T(8,128)S(1)}, f32[16,16,256]{2,0,1:T(8,128)S(1)}, u32[]{:S(2)}, u32[]{:S(2)}) collective-permute-start(f32[16,16,256]{2,0,1:T(8,128)S(1)} %bitcast_add_fusion.2), channel_id=1, source_target_pairs={{0,8},{4,0},{12,4},{20,12},{28,20},{24,28},{16,24},{8,16},{1,9},{5... | collective-permute-start | bytes 786440 | tf_op jit(solution)/shard_map/ppermute | solution.py:72
  274.7 8.3 %collective-permute-start.5 = (f32[16,16,256]{2,0,1:T(8,128)S(1)}, f32[16,16,256]{2,0,1:T(8,128)S(1)}, u32[]{:S(2)}, u32[]{:S(2)}) collective-permute-start(f32[16,16,256]{2,0,1:T(8,128)S(1)} %bitcast_add_fusion.9), channel_id=1, source_target_pairs={{0,4},{4,12},{12,20},{20,28},{28,24},{24,16},{16,8},{8,0},{1,5},{5... | collective-permute-start | bytes 786440 | tf_op jit(solution)/shard_map/ppermute | solution.py:72
  282.6 8.0 %collective-permute-start.13 = (f32[16,16,256]{2,0,1:T(8,128)S(1)}, f32[16,16,256]{2,0,1:T(8,128)S(1)}, u32[]{:S(2)}, u32[]{:S(2)}) collective-permute-start(f32[16,16,256]{2,0,1:T(8,128)S(1)} %bitcast_add_fusion.1), channel_id=1, source_target_pairs={{0,8},{4,0},{12,4},{20,12},{28,20},{24,28},{16,24},{8,16},{1,9},{5... | collective-permute-start | bytes 786440 | tf_op jit(solution)/shard_map/ppermute | solution.py:72
  284.0 7.7 %collective-permute-start.6 = (f32[16,16,256]{2,0,1:T(8,128)S(1)}, f32[16,16,256]{2,0,1:T(8,128)S(1)}, u32[]{:S(2)}, u32[]{:S(2)}) collective-permute-start(f32[16,16,256]{2,0,1:T(8,128)S(1)} %bitcast_add_fusion.8), channel_id=1, source_target_pairs={{0,4},{4,12},{12,20},{20,28},{28,24},{24,16},{16,8},{8,0},{1,5},{5... | collective-permute-start | bytes 786440 | tf_op jit(solution)/shard_map/ppermute | solution.py:72
Sparse Core Ops, SparseCore 0:
  13.1 88.9 all-gather.2
